TPU v7x, 512 devices: a whole 4x4x16 slice. The times are simulated.
512 devices in a mesh: phase: 16 (over x, z_hi), slab: 32 (over z_lo, y, core).
Axes of the slice: x: 4, y: 4, z: 16 (z_hi: 4, z_lo: 4; z = z_hi * 4 + z_lo), core: 2. Of those that a mesh axis runs over, the one named last changes fastest.
Arguments:
- pressure: float32 [2, 64, 32, 98304], P(None, 'phase', None, 'slab'), may hold values from -6 to 6
- mode_shapes: float32 [1024, 98304], P('phase', 'slab'), may hold values from -0.0390625 to 0.0390625
- point_weight: float32 [98304], P('slab'), may hold values from 0.5 to 2
- panel_order: int32 [8], replicated, may hold values from 0 to 7, each once
Outputs:
- influence: float32 [2, 64, 32, 1024], P(None, None, 'phase', 'slab')
Inputs may be any that keep to these rules, and one draw needn't show every extreme that they name: panel_order names each of 0 to 7 once.
All inputs are finite; a program needn't handle non-finite values.
Results may differ from a plain program's by a relative error of at most 0.00007.
Values sent between devices are 32-bit elements; how exact they have to be, the bound alone decides.
No kernel may reach another device: no remote copies, remote signals or barrier semaphores. Data moves between devices by JAX's collectives and lax.ppermute only.
A program may use at most 64 MiB of HBM per device.

v0:
```python
import math
import jax
import jax.numpy as jnp
from jax import lax
from jax.sharding import PartitionSpec as P


def blade_table(blades, count):
    phases = jnp.arange(count, dtype=jnp.int32)
    target = jnp.arange(blades, dtype=jnp.int32)
    index = target[:, None] * phases[None, :] % blades
    theta = index.astype(jnp.float32) * (2.0 * math.pi / blades)
    cosine = jnp.cos(theta)
    sine = jnp.sin(theta)
    upper = jnp.concatenate([cosine, -sine], axis=1)
    lower = jnp.concatenate([sine, cosine], axis=1)
    return jnp.concatenate([upper, lower], axis=0) * (1.0 / math.sqrt(blades))


def shards(pressure, mode_shapes, point_weight, panel_order):
    weighted = mode_shapes * point_weight[None, :]
    phase_dev = pressure.shape[1]
    excite = pressure.shape[2]
    rows = pressure.reshape(2 * phase_dev * excite, pressure.shape[3])
    partial_forces = lax.dot_general(
        rows,
        lax.all_gather(weighted, "phase", axis=0, tiled=True),
        (((1,), (1,)), ((), ())),
        precision=lax.Precision.HIGHEST,
        preferred_element_type=jnp.float32,
    )
    row_count = partial_forces.shape[0]
    panel_count = panel_order.shape[0]
    panels = partial_forces.reshape(row_count, panel_count, -1)
    selector = (panel_order[:, None] == jnp.arange(panel_count, dtype=jnp.int32)[None, :]).astype(
        jnp.float32
    )
    reordered = jnp.einsum(
        "rqc,pq->rpc", panels, selector, precision=lax.Precision.HIGHEST
    ).reshape(row_count, -1)
    slab_count = lax.axis_size("slab")
    total = lax.psum(reordered, "slab")
    keep_width = total.shape[1] // slab_count
    share = lax.dynamic_slice_in_dim(total, lax.axis_index("slab") * keep_width, keep_width, 1)
    mode_local = share.shape[1]
    forces = share.reshape(2, phase_dev, excite, mode_local)
    blades = phase_dev * lax.axis_size("phase")
    gathered = lax.all_to_all(forces, "phase", split_axis=2, concat_axis=1, tiled=True)
    table = blade_table(blades, blades)
    result = jnp.dot(
        table,
        gathered.reshape(2 * blades, -1),
        precision=lax.Precision.HIGHEST,
        preferred_element_type=jnp.float32,
    )
    result = result.reshape(2, blades, -1, mode_local)
    return result


def solution(mesh):
    placed = (P(None, "phase", None, "slab"), P("phase", "slab"), P("slab"), P())
    return jax.shard_map(
        shards,
        mesh=mesh,
        in_specs=placed,
        out_specs=P(None, None, "phase", "slab"),
        check_vma=False,
    )
```

profile of v0, /device:TPU:2, one launch (start us, length us, event | category | flops | bytes accessed | tf_op | source)
XLA Modules:
  0.0 662.7 jit_solution(11755668683219762363)
XLA Ops:
  6.5 2.3 broadcast_multiply_fusion
  8.8 0.0 all-reduce.2.cloned.1.call-start
  8.9 307.7 %all-gather.2.cloned.1.call-done = f32[1024,3072]{1,0:T(8,128)} async-done(((f32[64,3072]{1,0:T(8,128)}), f32[1024,3072]{1,0:T(8,128)}) %all-gather.2.cloned.1.call-update) | async-done | bytes 12582928 | tf_op jit(solution)/shard_map/all_gather | solution.py:27
  316.6 13.5 %fusion.12 = f32[1024,256]{1,0:T(8,128)} fusion(f32[1024,3072]{1,0:T(8,128)} %all-gather.2.cloned.1.call-done, f32[256,3072]{1,0:T(8,128)S(1)} %bitcast.31), kind=kOutput, calls=%fused_computation.19 | convolution fusion | flops 9663676416 | bytes 16777216 | tf_op jit(solution)/shard_map/dot_general | solution.py:25
  330.1 2.5 copy.13
  332.6 2.9 convolution_bitcast_fusion
  335.5 2.5 copy.20
  338.0 0.0 all-reduce.2.cloned.1.call-update
  338.1 0.1 fusion.6
  338.2 285.0 %all-reduce.2.cloned.1.call-done = f32[256,1024]{0,1:T(8,128)} async-done(((f32[256,1024]{0,1:T(8,128)}), f32[256,1024]{0,1:T(8,128)}) %all-reduce.2.cloned.1.call-update) | async-done | bytes 1048592 | tf_op jit(solution)/shard_map/psum | solution.py:42
  623.2 0.8 constant_dynamic-slice_fusion
  624.0 0.1 reshape.32
  624.1 0.1 copy.15
  624.3 0.8 reshape.37
  625.0 14.8 %all-to-all-start = ((f32[16,1,512]{2,1,0:T(1,128)}), f32[16,1,512]{2,1,0:T(1,128)S(1)}, u32[]{:S(2)}, u32[]{:S(2)}) async-start(f32[16,1,512]{2,1,0:T(1,128)} %reshape.37), calls=%async_computation | async-start | bytes 65536 | tf_op jit(solution)/shard_map/all_to_all | solution.py:48
  639.8 0.1 fusion.8
  639.9 0.1 maximum_multiply_fusion
  640.0 13.2 %all-to-all-done = f32[16,1,512]{2,1,0:T(1,128)S(1)} async-done(((f32[16,1,512]{2,1,0:T(1,128)}), f32[16,1,512]{2,1,0:T(1,128)S(1)}, u32[]{:S(2)}, u32[]{:S(2)}) %all-to-all-start) | async-done | bytes 32800 | tf_op jit(solution)/shard_map/all_to_all | solution.py:48
  653.2 0.5 broadcast.24
  653.7 0.7 reduce
  654.5 0.1 reshape.38
  654.7 0.1 reshape.33
  654.8 0.1 copy.18
  654.9 1.0 fusion.13
  (8 shorter events, 0.1 us)
Async XLA Ops:
  6.5 310.1 %copy-start = (f32[2,4,32,3072]{3,2,1,0:T(8,128)S(1)}, f32[2,4,32,3072]{3,2,1,0:T(8,128)}, u32[]{:S(2)}) copy-start(f32[2,4,32,3072]{3,2,1,0:T(8,128)} %param.4) | copy-start | bytes 9437188
  6.5 326.1 %copy-start.1 = (s32[8]{0:T(128)S(1)}, s32[8]{0:T(128)}, u32[]{:S(2)}) copy-start(s32[8]{0:T(128)} %param.7) | copy-start | bytes 100
  6.5 310.1 %all-gather.2.cloned.1.call-start = ((), (), s32[]{:S(2)}) async-start(), calls=%async_computation.1 | async-start | bytes 13369344 | tf_op jit(solution)/shard_map/all_gather | solution.py:27
  8.8 614.4 %all-reduce.2.cloned.1.call-start = ((), (), s32[]{:S(2)}) async-start(), calls=%async_computation.2 | async-start | bytes 2097152 | tf_op jit(solution)/shard_map/psum | solution.py:42
  625.0 28.2 %all-to-all-start = ((f32[16,1,512]{2,1,0:T(1,128)}), f32[16,1,512]{2,1,0:T(1,128)S(1)}, u32[]{:S(2)}, u32[]{:S(2)}) async-start(f32[16,1,512]{2,1,0:T(1,128)} %reshape.37), calls=%async_computation | async-start | bytes 65536 | tf_op jit(solution)/shard_map/all_to_all | solution.py:48
Sparse Core Ops, SparseCore 0:
  10.4 306.1 all-gather.1
  338.2 285.0 all-reduce.1
where the time goes:
time: 663 us
  waiting for transfers between devices  606 us (91%)
  matrix products  17.3 us (3%)
  starting transfers between devices  14.8 us (2%)
  between operations  13.5 us (2%)
  local copies, waits for them, and re-layouts  7.73 us (1%)
    all_gather x1, waiting for transfers between devices, shards(): lax.all_gather(weighted, 'phase', axis=0, tiled=True)  308 us
    psum x1, waiting for transfers between devices, shards(): total = lax.psum(reordered, 'slab')  285 us
    all_to_all x1, starting transfers between devices, shards(): lax.all_to_all(forces, 'phase', split_axis=2, concat_axis=1, tiled=True)  14.8 us
    dot_general x1, matrix products, shards(): lax.dot_general(rows, lax.all_gather(weighted, 'phase', axis=0, tiled=Tru...  13.5 us
  transfers between devices with their start and end apart: 3, of which 3 were waited for; matrix products, arithmetic and copies ran while one was open for 0% of the time, Pallas kernels for 0%

commit v1 on v0

--- a/solution.py
+++ b/solution.py
@@ -45,7 +45,10 @@
     mode_local = share.shape[1]
     forces = share.reshape(2, phase_dev, excite, mode_local)
     blades = phase_dev * lax.axis_size("phase")
-    gathered = lax.all_to_all(forces, "phase", split_axis=2, concat_axis=1, tiled=True)
+    gathered = jnp.concatenate(
+        lax.all_to_all(jnp.stack(jnp.split(forces, lax.axis_size("phase"), axis=2)), "phase", 0, 0),
+        axis=1,
+    )
     table = blade_table(blades, blades)
     result = jnp.dot(
         table,

time: 663 us -> 677 us (1.021)
  local copies, waits for them, and re-layouts: 7.73 us -> 22.2 us
    unnamed x6 -> x21, local copies, waits for them, and re-layouts: 0.88 us -> 12.5 us
where the time goes in v1:
time: 677 us
  waiting for transfers between devices  606 us (90%)
  local copies, waits for them, and re-layouts  22.2 us (3%)
  matrix products  17.3 us (3%)
  starting transfers between devices  14.9 us (2%)
  between operations  13.5 us (2%)
    all_gather x1, waiting for transfers between devices, shards(): lax.all_gather(weighted, 'phase', axis=0, tiled=True)  308 us
    psum x1, waiting for transfers between devices, shards(): total = lax.psum(reordered, 'slab')  285 us
    all_to_all x1, starting transfers between devices, shards(): lax.all_to_all(jnp.stack(jnp.split(forces, lax.axis_size('phase'), axis=2...  14.9 us
  transfers between devices with their start and end apart: 3, of which 3 were waited for; matrix products, arithmetic and copies ran while one was open for 0% of the time, Pallas kernels for 0%

profile of v1, /device:TPU:2, one launch (start us, length us, event | category | flops | bytes accessed | tf_op | source)
XLA Modules:
  0.0 677.0 jit_solution(8253058357911219698)
XLA Ops:
  6.5 2.3 broadcast_multiply_fusion
  8.9 307.7 %all-gather.2.cloned.1.call-done = f32[1024,3072]{1,0:T(8,128)} async-done(((f32[64,3072]{1,0:T(8,128)}), f32[1024,3072]{1,0:T(8,128)}) %all-gather.2.cloned.1.call-update) | async-done | bytes 12582928 | tf_op jit(solution)/shard_map/all_gather | solution.py:27
  316.6 13.5 %fusion.28 = f32[1024,256]{1,0:T(8,128)} fusion(f32[1024,3072]{1,0:T(8,128)} %all-gather.2.cloned.1.call-done, f32[256,3072]{1,0:T(8,128)S(1)} %bitcast.95), kind=kOutput, calls=%fused_computation.52 | convolution fusion | flops 9663676416 | bytes 16777216 | tf_op jit(solution)/shard_map/dot_general | solution.py:25
  330.1 2.6 copy.46
  332.6 2.9 convolution_bitcast_fusion
  335.5 2.5 copy.52
  338.2 284.8 %all-reduce.2.cloned.1.call-done = f32[256,1024]{0,1:T(8,128)} async-done(((f32[256,1024]{0,1:T(8,128)}), f32[256,1024]{0,1:T(8,128)}) %all-reduce.2.cloned.1.call-update) | async-done | bytes 1048592 | tf_op jit(solution)/shard_map/psum | solution.py:42
  624.6 0.8 fusion.14
  625.4 0.8 fusion.13
  626.2 0.8 fusion.12
  626.9 0.8 fusion.11
  627.7 0.8 fusion.10
  628.5 0.8 fusion.9
  629.3 0.8 fusion.8
  630.9 0.8 fusion.6
  631.6 0.8 fusion.5
  633.2 0.8 fusion.3
  634.0 0.8 fusion.2
  634.8 0.8 fusion.1
  635.6 0.8 fusion
  636.3 2.1 copy.48
  639.2 14.9 %all-to-all-start = ((f32[16,1,512]{2,1,0:T(1,128)}), f32[16,1,512]{2,1,0:T(1,128)S(1)}, u32[]{:S(2)}, u32[]{:S(2)}) async-start(f32[16,1,512]{2,1,0:T(1,128)} %reshape.36), calls=%async_computation | async-start | bytes 65536 | tf_op jit(solution)/shard_map/all_to_all | solution.py:49
  654.3 13.2 %all-to-all-done = f32[16,1,512]{2,1,0:T(1,128)S(1)} async-done(((f32[16,1,512]{2,1,0:T(1,128)}), f32[16,1,512]{2,1,0:T(1,128)S(1)}, u32[]{:S(2)}, u32[]{:S(2)}) %all-to-all-start) | async-done | bytes 32800 | tf_op jit(solution)/shard_map/all_to_all | solution.py:49
  669.2 1.0 fusion.29
  (24 shorter events, 5.9 us)
Async XLA Ops:
  6.5 310.1 %copy-start = (f32[2,4,32,3072]{3,2,1,0:T(8,128)S(1)}, f32[2,4,32,3072]{3,2,1,0:T(8,128)}, u32[]{:S(2)}) copy-start(f32[2,4,32,3072]{3,2,1,0:T(8,128)} %param.4) | copy-start | bytes 9437188
  6.5 310.1 %all-gather.2.cloned.1.call-start = ((), (), s32[]{:S(2)}) async-start(), calls=%async_computation.1 | async-start | bytes 13369344 | tf_op jit(solution)/shard_map/all_gather | solution.py:27
  8.8 614.2 %all-reduce.2.cloned.1.call-start = ((), (), s32[]{:S(2)}) async-start(), calls=%async_computation.2 | async-start | bytes 2097152 | tf_op jit(solution)/shard_map/psum | solution.py:42
  330.1 2.6 copy-start.1
  639.2 28.3 %all-to-all-start = ((f32[16,1,512]{2,1,0:T(1,128)}), f32[16,1,512]{2,1,0:T(1,128)S(1)}, u32[]{:S(2)}, u32[]{:S(2)}) async-start(f32[16,1,512]{2,1,0:T(1,128)} %reshape.36), calls=%async_computation | async-start | bytes 65536 | tf_op jit(solution)/shard_map/all_to_all | solution.py:49
Sparse Core Ops, SparseCore 0:
  10.4 306.1 all-gather.1
  338.2 284.8 all-reduce.1

commit v2 on v0

--- a/solution.py
+++ b/solution.py
@@ -24,7 +24,9 @@
     rows = pressure.reshape(2 * phase_dev * excite, pressure.shape[3])
     partial_forces = lax.dot_general(
         rows,
-        lax.all_gather(weighted, "phase", axis=0, tiled=True),
+        jnp.concatenate(
+            lax.all_to_all(jnp.stack([weighted] * lax.axis_size("phase")), "phase", 0, 0), axis=0
+        ),
         (((1,), (1,)), ((), ())),
         precision=lax.Precision.HIGHEST,
         preferred_element_type=jnp.float32,

time: 663 us -> 916 us (1.38)
  blocking collectives: 0 us -> 564 us
  waiting for transfers between devices: 606 us -> 297 us
    all_to_all x0 -> x1, blocking collectives: none -> 564 us  [shards(): lax.all_to_all(jnp.stack([weighted] * lax.axis_size('phase')), 'phase', 0...]
    all_gather x1 -> x0, waiting for transfers between devices: 308 us -> none  [shards(): lax.all_gather(weighted, 'phase', axis=0, tiled=True)]
  transfers between devices with their start and end apart: 3 -> 2, of which waited for: 3 -> 2; matrix products, arithmetic and copies ran while one was open for 0% -> 0% of each run, Pallas kernels for 0% -> 0%
where the time goes in v2:
time: 916 us
  blocking collectives  564 us (62%)
  waiting for transfers between devices  297 us (32%)
  matrix products  15.1 us (2%)
  starting transfers between devices  14.8 us (2%)
  between operations  13.5 us (1%)
  local copies, waits for them, and re-layouts  9.29 us (1%)
    all_to_all x1, blocking collectives, shards(): lax.all_to_all(jnp.stack([weighted] * lax.axis_size('phase')), 'phase', 0...  564 us
    psum x1, waiting for transfers between devices, shards(): total = lax.psum(reordered, 'slab')  284 us
  transfers between devices with their start and end apart: 2, of which 2 were waited for; matrix products, arithmetic and copies ran while one was open for 0% of the time, Pallas kernels for 0%

profile of v2, /device:TPU:2, one launch (start us, length us, event | category | flops | bytes accessed | tf_op | source)
XLA Modules:
  0.0 915.6 jit_solution(14277636013267403603)
XLA Ops:
  6.5 1.3 broadcast_multiply_fusion
  7.9 1.6 stack.2
  9.5 563.7 %all_to_all.20 = f32[16,64,3072]{2,1,0:T(8,128)S(1)} all-to-all(f32[16,64,3072]{2,1,0:T(8,128)S(1)} %stack.2), channel_id=1, replica_groups=mesh['phase'=16,'slab'=32] {'phase'}, dimensions={0} | all-to-all | bytes 25165824 | tf_op jit(solution)/shard_map/all_to_all | solution.py:28
  573.2 11.2 %fusion.12 = f32[1024,256]{1,0:T(8,128)} fusion(f32[1024,3072]{1,0:T(8,128)S(1)} %bitcast.33, f32[256,3072]{1,0:T(8,128)S(1)} %bitcast.32), kind=kOutput, calls=%fused_computation.19 | convolution fusion | flops 9663676416 | bytes 16777216 | tf_op jit(solution)/shard_map/dot_general | solution.py:25
  584.4 2.5 copy.13
  587.0 2.9 convolution_bitcast_fusion
  589.9 2.5 copy.20
  592.4 0.0 all-reduce.2.cloned.1.call-update
  592.4 0.1 fusion.6
  592.6 283.6 %all-reduce.2.cloned.1.call-done = f32[256,1024]{0,1:T(8,128)} async-done(((f32[256,1024]{0,1:T(8,128)}), f32[256,1024]{0,1:T(8,128)}) %all-reduce.2.cloned.1.call-update) | async-done | bytes 1048592 | tf_op jit(solution)/shard_map/psum | solution.py:44
  876.2 0.8 constant_dynamic-slice_fusion
  876.9 0.1 reshape.38
  877.0 0.1 copy.15
  877.2 0.8 reshape.43
  877.9 14.8 %all-to-all-start.1 = ((f32[16,1,512]{2,1,0:T(1,128)}), f32[16,1,512]{2,1,0:T(1,128)S(1)}, u32[]{:S(2)}, u32[]{:S(2)}) async-start(f32[16,1,512]{2,1,0:T(1,128)} %reshape.43), calls=%async_computation.1 | async-start | bytes 65536 | tf_op jit(solution)/shard_map/all_to_all | solution.py:50
  892.7 0.1 fusion.8
  892.8 0.1 maximum_multiply_fusion
  892.9 13.2 %all-to-all-done.1 = f32[16,1,512]{2,1,0:T(1,128)S(1)} async-done(((f32[16,1,512]{2,1,0:T(1,128)}), f32[16,1,512]{2,1,0:T(1,128)S(1)}, u32[]{:S(2)}, u32[]{:S(2)}) %all-to-all-start.1) | async-done | bytes 32800 | tf_op jit(solution)/shard_map/all_to_all | solution.py:50
  906.1 0.5 broadcast.26
  906.7 0.7 reduce
  907.4 0.1 reshape.44
  907.6 0.1 reshape.39
  907.7 0.1 copy.18
  907.8 1.0 fusion.13
  (7 shorter events, 0.1 us)
Async XLA Ops:
  6.5 566.7 %copy-start = (f32[2,4,32,3072]{3,2,1,0:T(8,128)S(1)}, f32[2,4,32,3072]{3,2,1,0:T(8,128)}, u32[]{:S(2)}) copy-start(f32[2,4,32,3072]{3,2,1,0:T(8,128)} %param.4) | copy-start | bytes 9437188
  6.5 869.6 %all-reduce.2.cloned.1.call-start = ((), (), s32[]{:S(2)}) async-start(), calls=%async_computation.2 | async-start | bytes 2097152 | tf_op jit(solution)/shard_map/psum | solution.py:44
  573.2 13.8 %copy-start.1 = (s32[8]{0:T(128)S(1)}, s32[8]{0:T(128)}, u32[]{:S(2)}) copy-start(s32[8]{0:T(128)} %param.7) | copy-start | bytes 100
  877.9 28.2 %all-to-all-start.1 = ((f32[16,1,512]{2,1,0:T(1,128)}), f32[16,1,512]{2,1,0:T(1,128)S(1)}, u32[]{:S(2)}, u32[]{:S(2)}) async-start(f32[16,1,512]{2,1,0:T(1,128)} %reshape.43), calls=%async_computation.1 | async-start | bytes 65536 | tf_op jit(solution)/shard_map/all_to_all | solution.py:50
Sparse Core Ops, SparseCore 0:
  592.5 283.5 all-reduce.1
